TPU v7x, 128 devices: a whole 4x4x4 slice. The times are simulated.
128 devices in a mesh: chan: 16 (over y_lo, z, core), band: 8 (over x, y_hi).
Axes of the slice: x: 4, y: 4 (y_hi: 2, y_lo: 2; y = y_hi * 2 + y_lo), z: 4, core: 2. Of those that a mesh axis runs over, the one named last changes fastest.
Arguments:
- raw: bfloat16 [128, 2560, 2747], P(('chan', 'band')), may hold values from -600 to 600
- offsets: int32 [128], P(('chan', 'band')), may hold values from 0 to 127
- taps: bfloat16 [63], replicated, may hold values from -0.75 to 0.75
- partner: int32 [2, 16], replicated, may hold values from 0 to 15, as said below
Outputs:
- cross: float32 [2, 2, 128, 2560, 160], P(None, None, 'band', 'chan')
Inputs may be any that keep to these rules, and one draw needn't show every extreme that they name: For each round r there is one number M of 1 to 15 with partner[r, a] = a xor M for every block a; the two rounds' numbers differ.
All inputs are finite; a program needn't handle non-finite values.
Results may differ from a plain program's by a relative error of at most 0.0041.
Values may be sent and summed in bfloat16 or wider, within the bound.
No kernel may reach another device: no remote copies, remote signals or barrier semaphores. Data moves between devices by JAX's collectives and lax.ppermute only.
A program may use at most 128 MiB of HBM per device.

v0:
```python
import math

import jax
import numpy as np
import jax.numpy as jnp
from jax import lax
from jax.sharding import PartitionSpec as P

DEC = 10
TAPS = 63
W = 256
NF = 128
HALF = 32


def mean_matrix(length, half):
    rows = jnp.arange(length, dtype=jnp.int32)[:, None]
    cols = jnp.arange(length, dtype=jnp.int32)[None, :]
    begins = jnp.clip(cols - half, 0, length - 2 * half - 1)
    inside = (rows >= begins) & (rows <= begins + 2 * half)
    return inside.astype(jnp.float32)


def dft_table(length, bins):
    samples = jnp.arange(length, dtype=jnp.int32)[:, None]
    freqs = jnp.arange(bins, dtype=jnp.int32)[None, :]
    phase = samples * freqs % length
    angle = phase.astype(jnp.float32) * (2.0 * math.pi / length)
    return jnp.concatenate([jnp.cos(angle), -jnp.sin(angle)], axis=1)


def filter_table(taps, phases):
    padded = jnp.pad(taps, (0, phases * DEC - TAPS))
    grid = padded.reshape(phases, DEC)
    rows = jnp.arange(W + phases - 1, dtype=jnp.int32)[:, None]
    cols = jnp.arange(W, dtype=jnp.int32)[None, :]
    onehot = (
        (rows - cols)[None, :, :] == jnp.arange(phases, dtype=jnp.int32)[:, None, None]
    ).astype(jnp.bfloat16)
    table = jnp.einsum("jqn,jr->qrn", onehot, grid, preferred_element_type=jnp.float32)
    return table.reshape((W + phases - 1) * DEC, W).astype(jnp.bfloat16)


def window_spectrum(segment, offset, table, level_matrix, transform, blocks, bands):
    span = table.shape[0]
    piece = lax.dynamic_slice_in_dim(segment, offset, span, 1)
    decimated = jnp.dot(piece, table, preferred_element_type=jnp.float32)
    level = jnp.dot(jnp.abs(decimated), level_matrix, precision=lax.Precision.HIGH) / (
        2 * HALF + 1
    )
    normed = decimated / (level + 1e-05)
    channels = segment.shape[0]
    ordered = np.ascontiguousarray(
        transform.reshape(W, 2, bands, NF // bands).transpose(2, 1, 3, 0).reshape(2 * NF, W)
    )
    spectrum = jnp.einsum(
        "akn,ain->aki",
        jnp.broadcast_to(ordered[None], (blocks, 2 * NF, W)),
        normed.reshape(blocks, channels // blocks, W),
        precision=lax.Precision.HIGH,
    )
    return spectrum.reshape(blocks, bands, 2, NF // bands, channels // blocks).astype(jnp.bfloat16)


def body(raw, offsets, taps, partner):
    phases = (TAPS + DEC - 1) // DEC
    table = filter_table(taps, phases)
    rows_np = np.arange(W)[:, None]
    begins_np = np.clip(np.arange(W)[None, :] - HALF, 0, W - 2 * HALF - 1)
    level_matrix = ((rows_np >= begins_np) & (rows_np <= begins_np + 2 * HALF)).astype(np.float32)
    phase = (np.arange(W)[:, None] * np.arange(NF)[None, :]) % W
    angle = phase.astype(np.float32) * np.float32(2.0 * math.pi / W)
    transform = np.concatenate([np.cos(angle), -np.sin(angle)], axis=1).astype(np.float32)
    chan_count = lax.axis_size("chan")
    band_count = lax.axis_size("band")
    spectrum = window_spectrum(
        raw[0], offsets[0], table, level_matrix, transform, chan_count, band_count
    )
    _, _, part_count, bins, width = spectrum.shape
    arranged = spectrum.transpose(2, 3, 4, 0, 1).reshape(
        part_count, bins, width, chan_count * band_count
    )
    local = lax.all_to_all(arranged, ("chan", "band"), split_axis=3, concat_axis=3, tiled=True)

    def exchange(rows, number):
        def branch(shift):
            pairs = [(a, a ^ shift) for a in range(chan_count)]
            return lambda x: lax.ppermute(x, "chan", pairs)

        branches = [branch(shift) for shift in range(1, chan_count)]
        return lax.switch(number - 1, branches, rows)

    first_other = exchange(local, partner[0, 0])
    second_other = exchange(local, partner[1, 0])
    factor = 1.0 / (W * math.sqrt(local.shape[3]))
    columns = []
    for other_rows in (first_other, second_other):
        columns.append(other_rows)
        columns.append(jnp.stack([-other_rows[1], other_rows[0]]))
    mixed = jnp.stack(columns)
    own = jnp.broadcast_to(local[None], mixed.shape)
    product = jnp.einsum("qpfiw,qpfjw->qfij", own, mixed, preferred_element_type=jnp.float32)
    return (product * factor).reshape(2, 2, bins, width, width)


def solution(mesh):
    return jax.shard_map(
        body,
        mesh=mesh,
        in_specs=(P(("chan", "band"), None, None), P(("chan", "band")), P(), P()),
        out_specs=P(None, None, "band", "chan", None),
        check_vma=False,
    )
```

profile of v0, /device:TPU:2, one launch (start us, length us, event | category | flops | bytes accessed | tf_op | source)
XLA Modules:
  0.0 139.0 jit_solution(13623485699681768230)
XLA Ops:
  0.7 0.7 pad.4
  1.3 0.1 reshape.44
  1.4 0.8 convert_bitcast_fusion
  2.2 0.5 convert_element_type.23
  2.7 0.0 copy-start.3
  2.7 7.2 %fusion = f32[2560,256]{1,0:T(8,128)S(1)} fusion(bf16[2620,256]{1,0:T(8,128)(2,1)S(1)} %convert_element_type.23, bf16[1,2560,2747]{1,2,0:T(8,128)(2,1)} %param.36, s32[]{:T(128)S(6)} %select_n.3), kind=kOutput, calls=%fused_computation | convolution fusion | flops 3434086400 | bytes 17397764 | tf_op jit(solution)/shard_map/dot_general | solution.py:47
  9.9 0.0 copy-done.3
  9.9 0.0 copy-start.1
  9.9 1.2 fusion.12
  11.2 0.0 copy-done.1
  11.2 2.3 %fusion.23 = bf16[16,256,160]{1,2,0:T(8,128)(2,1)S(1)} fusion(f32[16,160,256]{2,1,0:T(8,128)S(1)} %bitcast.40, f32[256,256]{1,0:T(8,128)S(1)} %copy-done.1), kind=kOutput, calls=%fused_computation.23 | convolution fusion | flops 1007288320 | bytes 4194304 | tf_op jit(solution)/shard_map/akn,ain->aki/dot_general | solution.py:56
  13.5 2.9 %copy.54 = bf16[16,256,160]{2,1,0:T(8,128)(2,1)} copy(bf16[16,256,160]{1,2,0:T(8,128)(2,1)S(1)} %fusion.23) | data formatting | bytes 2621440 | tf_op jit(solution)/shard_map/convert_element_type | solution.py:62
  16.3 0.0 copy-start.2
  16.3 10.5 %all-to-all-start = ((bf16[2,16,160,128]{2,1,0,3:T(8,128)(2,1)}), bf16[2,16,160,128]{2,1,0,3:T(8,128)(2,1)S(1)}, u32[]{:S(2)}, u32[]{:S(2)}) async-start(bf16[2,16,160,128]{2,1,0,3:T(8,128)(2,1)} %bitcast.37), calls=%async_computation | async-start | bytes 4194304 | tf_op jit(solution)/shard_map/all_to_all | solution.py:83
  26.9 0.0 copy-done.2
  26.9 0.5 fusion.29
  28.7 27.0 %all-to-all-done = bf16[2,16,160,128]{2,1,0,3:T(8,128)(2,1)S(1)} async-done(((bf16[2,16,160,128]{2,1,0,3:T(8,128)(2,1)}), bf16[2,16,160,128]{2,1,0,3:T(8,128)(2,1)S(1)}, u32[]{:S(2)}, u32[]{:S(2)}) %all-to-all-start) | async-done | bytes 1310752 | tf_op jit(solution)/shard_map/all_to_all | solution.py:83
  55.7 2.0 %copy.58 = bf16[2,16,160,128]{3,2,1,0:T(8,128)(2,1)S(1)} copy(bf16[2,16,160,128]{2,1,0,3:T(8,128)(2,1)S(1)} %all-to-all-done) | data formatting | bytes 2621440 | tf_op jit(solution)/shard_map/all_to_all | solution.py:83
  57.7 33.1 %conditional.3 = (bf16[2,16,160,128]{3,2,1,0:T(8,128)(2,1)}) conditional(s32[]{:T(128)} %bitcast.11, bf16[2,16,160,128]{3,2,1,0:T(8,128)(2,1)S(1)} %copy.58, bf16[2,16,160,128]{3,2,1,0:T(8,128)(2,1)S(1)} %copy.58, bf16[2,16,160,128]{3,2,1,0:T(8,128)(2,1)S(1)} %copy.58, ...), branch_computations={%region_15.16_spmd, %region_16.17_spmd, %region_17.18_spmd, %regio... | conditional | bytes 5242928 | solution.py:91
  57.7 0.6 collective-permute-start.29
  58.4 32.4 %collective-permute-done.29 = bf16[2,16,160,128]{3,2,1,0:T(8,128)(2,1)} collective-permute-done((bf16[2,16,160,128]{3,2,1,0:T(8,128)(2,1)S(1)}, bf16[2,16,160,128]{3,2,1,0:T(8,128)(2,1)}, u32[]{:S(2)}, u32[]{:S(2)}) %collective-permute-start.29) | collective-permute-done | bytes 1310752 | tf_op jit(solution)/shard_map/cond/branch_14_fun/ppermute | solution.py:88
  90.7 32.7 %conditional.2 = (bf16[2,16,160,128]{3,2,1,0:T(8,128)(2,1)}) conditional(s32[]{:T(128)} %bitcast.8, bf16[2,16,160,128]{3,2,1,0:T(8,128)(2,1)S(1)} %copy.58, bf16[2,16,160,128]{3,2,1,0:T(8,128)(2,1)S(1)} %copy.58, bf16[2,16,160,128]{3,2,1,0:T(8,128)(2,1)S(1)} %copy.58, ...), branch_computations={%region_0.1_spmd, %region_1.2_spmd, %region_2.3_spmd, %region_3.4_... | conditional | bytes 5242928 | solution.py:91
  90.7 0.0 collective-permute-start.4
  90.8 32.6 %collective-permute-done.4 = bf16[2,16,160,128]{3,2,1,0:T(8,128)(2,1)} collective-permute-done((bf16[2,16,160,128]{3,2,1,0:T(8,128)(2,1)S(1)}, bf16[2,16,160,128]{3,2,1,0:T(8,128)(2,1)}, u32[]{:S(2)}, u32[]{:S(2)}) %collective-permute-start.4) | collective-permute-done | bytes 1310752 | tf_op jit(solution)/shard_map/cond/branch_4_fun/ppermute | solution.py:88
  123.4 1.4 %copy.101 = bf16[2,16,160,128]{3,2,0,1:T(8,128)(2,1)S(1)} copy(bf16[2,16,160,128]{3,2,1,0:T(8,128)(2,1)} %get-tuple-element.79) | data formatting | bytes 2621440 | tf_op jit(solution)/shard_map/cond | solution.py:91
  124.9 1.4 %copy.100 = bf16[2,16,160,128]{3,2,0,1:T(8,128)(2,1)S(1)} copy(bf16[2,16,160,128]{3,2,1,0:T(8,128)(2,1)} %get-tuple-element.80) | data formatting | bytes 2621440 | tf_op jit(solution)/shard_map/cond | solution.py:91
  126.3 0.0 copy-start
  126.3 1.1 copy-done
  127.4 0.1 slice_negate_fusion
  127.5 0.1 slice_negate_fusion.1
  127.6 1.7 %maximum_bitcast_fusion = (bf16[1,2,16,160,128]{4,3,1,2,0:T(8,128)(2,1)}, bf16[1,2,16,160,128]{4,3,1,2,0:T(8,128)(2,1)}) fusion(bf16[1,16,160,128]{3,2,0,1:T(8,128)(2,1)S(1)} %get-tuple-element.70, bf16[1,16,160,128]{3,2,0,1:T(8,128)(2,1)S(1)} %get-tuple-element.69, bf16[1,16,160,128]{3,2,0,1:T(8,128)(2,1)S(1)} %get-tuple-element.74, ...), kind=kLoop, calls=%fused_computation.24 | loop fusion | flops 1310720 | bytes 5242880 | tf_op jit(solution)/shard_map/stack | solution.py:100
  129.4 2.9 %copy.57 = bf16[2,16,160,128]{3,2,0,1:T(8,128)(2,1)} copy(bf16[2,16,160,128]{2,1,0,3:T(8,128)(2,1)S(1)} %all-to-all-done) | data formatting | bytes 2621440 | tf_op jit(solution)/shard_map/all_to_all | solution.py:83
  132.2 6.7 %bitcast_multiply_fusion = f32[4,16,160,160]{3,2,1,0:T(8,128)} fusion(bf16[1,2,16,160,128]{4,3,1,2,0:T(8,128)(2,1)} %get-tuple-element.78, bf16[1,2,16,160,128]{4,3,1,2,0:T(8,128)(2,1)} %bitcast.39, bf16[1,2,16,160,128]{4,3,1,2,0:T(8,128)(2,1)} %get-tuple-element.77, bf16[1,2,16,160,128]{4,3,1,2,0:T(8,128)(2,1)S(1)} %bitcast.38, ...), kind=kOutput, calls=%fused_computation.3 | convolution fusion | flops 848363520 | bytes 13107200 | tf_op jit(solution)/shard_map/qpfiw,qpfjw->qfij/dot_general | solution.py:102
  (1 shorter events, 0.0 us)
Async XLA Ops:
  2.7 7.2 %copy-start.3 = (f32[256,256]{1,0:T(8,128)S(1)}, f32[256,256]{1,0:T(8,128)}, u32[]{:S(2)}) copy-start(f32[256,256]{1,0:T(8,128)} %constant.31.clone) | copy-start | bytes 786436
  9.9 1.2 copy-start.1
  16.3 10.5 %copy-start.2 = (s32[2,16]{1,0:T(2,128)S(1)}, s32[2,16]{1,0:T(2,128)}, u32[]{:S(2)}) copy-start(s32[2,16]{1,0:T(2,128)} %param.39) | copy-start | bytes 388
  16.3 39.3 %all-to-all-start = ((bf16[2,16,160,128]{2,1,0,3:T(8,128)(2,1)}), bf16[2,16,160,128]{2,1,0,3:T(8,128)(2,1)S(1)}, u32[]{:S(2)}, u32[]{:S(2)}) async-start(bf16[2,16,160,128]{2,1,0,3:T(8,128)(2,1)} %bitcast.37), calls=%async_computation | async-start | bytes 4194304 | tf_op jit(solution)/shard_map/all_to_all | solution.py:83
  57.7 33.0 %collective-permute-start.29 = (bf16[2,16,160,128]{3,2,1,0:T(8,128)(2,1)S(1)}, bf16[2,16,160,128]{3,2,1,0:T(8,128)(2,1)}, u32[]{:S(2)}, u32[]{:S(2)}) collective-permute-start(bf16[2,16,160,128]{3,2,1,0:T(8,128)(2,1)S(1)} %param.29), channel_id=1, source_target_pairs={{0,120},{8,112},{16,104},{24,96},{32,88},{40,80},{48,72},{56,64},{... | collective-permute-start | bytes 3932168 | tf_op jit(solution)/shard_map/cond/branch_14_fun/ppermute | solution.py:88
  90.7 32.7 %collective-permute-start.4 = (bf16[2,16,160,128]{3,2,1,0:T(8,128)(2,1)S(1)}, bf16[2,16,160,128]{3,2,1,0:T(8,128)(2,1)}, u32[]{:S(2)}, u32[]{:S(2)}) collective-permute-start(bf16[2,16,160,128]{3,2,1,0:T(8,128)(2,1)S(1)} %param.4), channel_id=1, source_target_pairs={{0,40},{8,32},{16,56},{24,48},{32,8},{40,0},{48,24},{56,16},{64,10... | collective-permute-start | bytes 3932168 | tf_op jit(solution)/shard_map/cond/branch_4_fun/ppermute | solution.py:88
  126.3 1.1 copy-start
where the time goes:
time: 138 us; the launch traced here: 139 us
  waiting for transfers between devices  92.1 us (67%)
  matrix products  18.2 us (13%)
  local copies, waits for them, and re-layouts  13.5 us (10%)
  starting transfers between devices  11.2 us (8%)
  between operations  2.01 us (1%)
  other arithmetic  2 us (1%)
    ppermute x2, waiting for transfers between devices, branch(): return lambda x: lax.ppermute(x, 'chan', pairs)  65 us
    all_to_all x1, waiting for transfers between devices, body(): lax.all_to_all(arranged, ('chan', 'band'), split_axis=3, concat_axis=3, t...  27 us
    all_to_all x1, starting transfers between devices, body(): lax.all_to_all(arranged, ('chan', 'band'), split_axis=3, concat_axis=3, t...  10.5 us
    dot_general x1, matrix products, window_spectrum(): decimated = jnp.dot(piece, table, preferred_element_type=jnp.float32)  7.19 us
    dot_general x1, matrix products, body(): jnp.einsum('qpfiw,qpfjw->qfij', own, mixed, preferred_element_type=jnp.fl...  6.74 us
    all_to_all x2, local copies, waits for them, and re-layouts, body(): lax.all_to_all(arranged, ('chan', 'band'), split_axis=3, concat_axis=3, t...  4.87 us
    convert_element_type x1, local copies, waits for them, and re-layouts, window_spectrum(): spectrum.reshape(blocks, bands, 2, NF // bands, channels // blocks)  2.89 us
    cond x2, local copies, waits for them, and re-layouts, exchange(): return lax.switch(number - 1, branches, rows)  2.88 us
  transfers between devices with their start and end apart: 3, of which 3 were waited for; matrix products, arithmetic and copies ran while one was open for 0% of the time, Pallas kernels for 0%

commit v1 on v0

--- a/solution.py
+++ b/solution.py
@@ -45,9 +45,14 @@
     span = table.shape[0]
     piece = lax.dynamic_slice_in_dim(segment, offset, span, 1)
     decimated = jnp.dot(piece, table, preferred_element_type=jnp.float32)
-    level = jnp.dot(jnp.abs(decimated), level_matrix, precision=lax.Precision.HIGH) / (
-        2 * HALF + 1
-    )
+    size = jnp.abs(decimated)
+    high = size.astype(jnp.bfloat16)
+    low = (size - high.astype(jnp.float32)).astype(jnp.bfloat16)
+    ones = level_matrix.astype(jnp.bfloat16)
+    level = (
+        jnp.dot(high, ones, preferred_element_type=jnp.float32)
+        + jnp.dot(low, ones, preferred_element_type=jnp.float32)
+    ) / (2 * HALF + 1)
     normed = decimated / (level + 1e-05)
     channels = segment.shape[0]
     ordered = np.ascontiguousarray(

time: 138 us -> 137 us (level); the launches traced: 139 us -> 135 us
  waiting for transfers between devices: 92.1 us -> 86.7 us
  starting transfers between devices: 11.2 us -> 12.7 us
    ppermute x2, waiting for transfers between devices: 65 us -> 59.7 us  [branch(): return lambda x: lax.ppermute(x, 'chan', pairs)]
    ppermute x2, starting transfers between devices: 0.65 us -> 2.18 us  [branch(): return lambda x: lax.ppermute(x, 'chan', pairs)]
where the time goes in v1:
time: 137 us; the launch traced here: 135 us
  waiting for transfers between devices  86.7 us (63%)
  matrix products  18.4 us (13%)
  local copies, waits for them, and re-layouts  13.5 us (10%)
  starting transfers between devices  12.7 us (9%)
  other arithmetic  2 us (1%)
  between operations  2 us (1%)
    ppermute x2, waiting for transfers between devices, branch(): return lambda x: lax.ppermute(x, 'chan', pairs)  59.7 us
    all_to_all x1, waiting for transfers between devices, body(): lax.all_to_all(arranged, ('chan', 'band'), split_axis=3, concat_axis=3, t...  27 us
    all_to_all x1, starting transfers between devices, body(): lax.all_to_all(arranged, ('chan', 'band'), split_axis=3, concat_axis=3, t...  10.5 us
    dot_general x1, matrix products, window_spectrum(): decimated = jnp.dot(piece, table, preferred_element_type=jnp.float32)  7.18 us
    dot_general x1, matrix products, body(): jnp.einsum('qpfiw,qpfjw->qfij', own, mixed, preferred_element_type=jnp.fl...  6.74 us
    all_to_all x2, local copies, waits for them, and re-layouts, body(): lax.all_to_all(arranged, ('chan', 'band'), split_axis=3, concat_axis=3, t...  4.87 us
    convert_element_type x1, local copies, waits for them, and re-layouts, window_spectrum(): spectrum.reshape(blocks, bands, 2, NF // bands, channels // blocks)  2.89 us
    cond x2, local copies, waits for them, and re-layouts, exchange(): return lax.switch(number - 1, branches, rows)  2.88 us
  transfers between devices with their start and end apart: 3, of which 3 were waited for; matrix products, arithmetic and copies ran while one was open for 0% of the time, Pallas kernels for 0%

profile of v1, /device:TPU:2, one launch (start us, length us, event | category | flops | bytes accessed | tf_op | source)
XLA Modules:
  0.0 135.4 jit_solution(2430251545010808483)
XLA Ops:
  0.7 0.7 pad.4
  1.3 0.1 reshape.44
  1.4 0.8 convert_bitcast_fusion
  2.2 0.5 convert_element_type.32
  2.7 0.0 copy-start.2
  2.7 7.2 %fusion = f32[2560,256]{1,0:T(8,128)S(1)} fusion(bf16[2620,256]{1,0:T(8,128)(2,1)S(1)} %convert_element_type.32, bf16[1,2560,2747]{1,2,0:T(8,128)(2,1)} %param.36, s32[]{:T(128)S(6)} %select_n.3), kind=kOutput, calls=%fused_computation | convolution fusion | flops 3434086400 | bytes 17397764 | tf_op jit(solution)/shard_map/dot_general | solution.py:47
  9.9 0.0 copy-done.2
  9.9 0.5 fusion.20
  10.5 0.0 copy-start.1
  10.5 0.9 fusion.13
  11.4 0.1 copy-done.1
  11.4 2.3 %fusion.24 = bf16[16,256,160]{1,2,0:T(8,128)(2,1)S(1)} fusion(f32[16,160,256]{2,1,0:T(8,128)S(1)} %bitcast.41, f32[256,256]{1,0:T(8,128)S(1)} %copy-done.1), kind=kOutput, calls=%fused_computation.26 | convolution fusion | flops 1007288320 | bytes 4194304 | tf_op jit(solution)/shard_map/akn,ain->aki/dot_general | solution.py:61
  13.7 2.9 %copy.54 = bf16[16,256,160]{2,1,0:T(8,128)(2,1)} copy(bf16[16,256,160]{1,2,0:T(8,128)(2,1)S(1)} %fusion.24) | data formatting | bytes 2621440 | tf_op jit(solution)/shard_map/convert_element_type | solution.py:67
  16.6 0.0 copy-start.3
  16.6 10.5 %all-to-all-start = ((bf16[2,16,160,128]{2,1,0,3:T(8,128)(2,1)}), bf16[2,16,160,128]{2,1,0,3:T(8,128)(2,1)S(1)}, u32[]{:S(2)}, u32[]{:S(2)}) async-start(bf16[2,16,160,128]{2,1,0,3:T(8,128)(2,1)} %bitcast.38), calls=%async_computation | async-start | bytes 4194304 | tf_op jit(solution)/shard_map/all_to_all | solution.py:88
  27.1 0.0 copy-done.3
  27.1 0.5 fusion.30
  28.9 27.0 %all-to-all-done = bf16[2,16,160,128]{2,1,0,3:T(8,128)(2,1)S(1)} async-done(((bf16[2,16,160,128]{2,1,0,3:T(8,128)(2,1)}), bf16[2,16,160,128]{2,1,0,3:T(8,128)(2,1)S(1)}, u32[]{:S(2)}, u32[]{:S(2)}) %all-to-all-start) | async-done | bytes 1310752 | tf_op jit(solution)/shard_map/all_to_all | solution.py:88
  55.9 2.0 %copy.58 = bf16[2,16,160,128]{3,2,1,0:T(8,128)(2,1)S(1)} copy(bf16[2,16,160,128]{2,1,0,3:T(8,128)(2,1)S(1)} %all-to-all-done) | data formatting | bytes 2621440 | tf_op jit(solution)/shard_map/all_to_all | solution.py:88
  57.9 30.4 %conditional.3 = (bf16[2,16,160,128]{3,2,1,0:T(8,128)(2,1)}) conditional(s32[]{:T(128)} %bitcast.11, bf16[2,16,160,128]{3,2,1,0:T(8,128)(2,1)S(1)} %copy.58, bf16[2,16,160,128]{3,2,1,0:T(8,128)(2,1)S(1)} %copy.58, bf16[2,16,160,128]{3,2,1,0:T(8,128)(2,1)S(1)} %copy.58, ...), branch_computations={%region_15.16_spmd, %region_16.17_spmd, %region_17.18_spmd, %regio... | conditional | bytes 5242928 | solution.py:96
  57.9 0.7 collective-permute-start.22
  58.6 29.6 %collective-permute-done.22 = bf16[2,16,160,128]{3,2,1,0:T(8,128)(2,1)} collective-permute-done((bf16[2,16,160,128]{3,2,1,0:T(8,128)(2,1)S(1)}, bf16[2,16,160,128]{3,2,1,0:T(8,128)(2,1)}, u32[]{:S(2)}, u32[]{:S(2)}) %collective-permute-start.22) | collective-permute-done | bytes 1310752 | tf_op jit(solution)/shard_map/cond/branch_7_fun/ppermute | solution.py:93
  88.2 31.5 %conditional.2 = (bf16[2,16,160,128]{3,2,1,0:T(8,128)(2,1)}) conditional(s32[]{:T(128)} %bitcast.8, bf16[2,16,160,128]{3,2,1,0:T(8,128)(2,1)S(1)} %copy.58, bf16[2,16,160,128]{3,2,1,0:T(8,128)(2,1)S(1)} %copy.58, bf16[2,16,160,128]{3,2,1,0:T(8,128)(2,1)S(1)} %copy.58, ...), branch_computations={%region_0.1_spmd, %region_1.2_spmd, %region_2.3_spmd, %region_3.4_... | conditional | bytes 5242928 | solution.py:96
  88.2 1.5 %collective-permute-start.13 = (bf16[2,16,160,128]{3,2,1,0:T(8,128)(2,1)S(1)}, bf16[2,16,160,128]{3,2,1,0:T(8,128)(2,1)}, u32[]{:S(2)}, u32[]{:S(2)}) collective-permute-start(bf16[2,16,160,128]{3,2,1,0:T(8,128)(2,1)S(1)} %param.13), channel_id=1, source_target_pairs={{0,112},{8,120},{16,96},{24,104},{32,80},{40,88},{48,64},{56,72},{... | collective-permute-start | bytes 3932168 | tf_op jit(solution)/shard_map/cond/branch_13_fun/ppermute | solution.py:93
  89.7 30.1 %collective-permute-done.13 = bf16[2,16,160,128]{3,2,1,0:T(8,128)(2,1)} collective-permute-done((bf16[2,16,160,128]{3,2,1,0:T(8,128)(2,1)S(1)}, bf16[2,16,160,128]{3,2,1,0:T(8,128)(2,1)}, u32[]{:S(2)}, u32[]{:S(2)}) %collective-permute-start.13) | collective-permute-done | bytes 1310752 | tf_op jit(solution)/shard_map/cond/branch_13_fun/ppermute | solution.py:93
  119.8 1.4 %copy.101 = bf16[2,16,160,128]{3,2,0,1:T(8,128)(2,1)S(1)} copy(bf16[2,16,160,128]{3,2,1,0:T(8,128)(2,1)} %get-tuple-element.79) | data formatting | bytes 2621440 | tf_op jit(solution)/shard_map/cond | solution.py:96
  121.2 1.4 %copy.100 = bf16[2,16,160,128]{3,2,0,1:T(8,128)(2,1)S(1)} copy(bf16[2,16,160,128]{3,2,1,0:T(8,128)(2,1)} %get-tuple-element.80) | data formatting | bytes 2621440 | tf_op jit(solution)/shard_map/cond | solution.py:96
  122.7 0.0 copy-start
  122.7 1.1 copy-done
  123.7 0.1 slice_negate_fusion
  123.9 0.1 slice_negate_fusion.1
  124.0 1.7 %maximum_bitcast_fusion = (bf16[1,2,16,160,128]{4,3,1,2,0:T(8,128)(2,1)}, bf16[1,2,16,160,128]{4,3,1,2,0:T(8,128)(2,1)}) fusion(bf16[1,16,160,128]{3,2,0,1:T(8,128)(2,1)S(1)} %get-tuple-element.70, bf16[1,16,160,128]{3,2,0,1:T(8,128)(2,1)S(1)} %get-tuple-element.69, bf16[1,16,160,128]{3,2,0,1:T(8,128)(2,1)S(1)} %get-tuple-element.74, ...), kind=kLoop, calls=%fused_computation.27 | loop fusion | flops 1310720 | bytes 5242880 | tf_op jit(solution)/shard_map/stack | solution.py:105
  125.7 2.9 %copy.57 = bf16[2,16,160,128]{3,2,0,1:T(8,128)(2,1)} copy(bf16[2,16,160,128]{2,1,0,3:T(8,128)(2,1)S(1)} %all-to-all-done) | data formatting | bytes 2621440 | tf_op jit(solution)/shard_map/all_to_all | solution.py:88
  128.6 6.7 %bitcast_multiply_fusion = f32[4,16,160,160]{3,2,1,0:T(8,128)} fusion(bf16[1,2,16,160,128]{4,3,1,2,0:T(8,128)(2,1)} %get-tuple-element.78, bf16[1,2,16,160,128]{4,3,1,2,0:T(8,128)(2,1)} %bitcast.40, bf16[1,2,16,160,128]{4,3,1,2,0:T(8,128)(2,1)} %get-tuple-element.77, bf16[1,2,16,160,128]{4,3,1,2,0:T(8,128)(2,1)S(1)} %bitcast.39, ...), kind=kOutput, calls=%fused_computation.3 | convolution fusion | flops 848363520 | bytes 13107200 | tf_op jit(solution)/shard_map/qpfiw,qpfjw->qfij/dot_general | solution.py:107
  (1 shorter events, 0.0 us)
Async XLA Ops:
  2.7 7.2 %copy-start.2 = (bf16[256,256]{1,0:T(8,128)(2,1)S(1)}, bf16[256,256]{1,0:T(8,128)(2,1)}, u32[]{:S(2)}) copy-start(bf16[256,256]{1,0:T(8,128)(2,1)} %constant.31.clone) | copy-start | bytes 393220
  10.5 1.0 copy-start.1
  16.6 10.5 %copy-start.3 = (s32[2,16]{1,0:T(2,128)S(1)}, s32[2,16]{1,0:T(2,128)}, u32[]{:S(2)}) copy-start(s32[2,16]{1,0:T(2,128)} %param.39) | copy-start | bytes 388
  16.6 39.3 %all-to-all-start = ((bf16[2,16,160,128]{2,1,0,3:T(8,128)(2,1)}), bf16[2,16,160,128]{2,1,0,3:T(8,128)(2,1)S(1)}, u32[]{:S(2)}, u32[]{:S(2)}) async-start(bf16[2,16,160,128]{2,1,0,3:T(8,128)(2,1)} %bitcast.38), calls=%async_computation | async-start | bytes 4194304 | tf_op jit(solution)/shard_map/all_to_all | solution.py:88
  57.9 30.4 %collective-permute-start.22 = (bf16[2,16,160,128]{3,2,1,0:T(8,128)(2,1)S(1)}, bf16[2,16,160,128]{3,2,1,0:T(8,128)(2,1)}, u32[]{:S(2)}, u32[]{:S(2)}) collective-permute-start(bf16[2,16,160,128]{3,2,1,0:T(8,128)(2,1)S(1)} %param.22), channel_id=1, source_target_pairs={{0,64},{8,72},{16,80},{24,88},{32,96},{40,104},{48,112},{56,120},{... | collective-permute-start | bytes 3932168 | tf_op jit(solution)/shard_map/cond/branch_7_fun/ppermute | solution.py:93
  88.2 31.5 %collective-permute-start.13 = (bf16[2,16,160,128]{3,2,1,0:T(8,128)(2,1)S(1)}, bf16[2,16,160,128]{3,2,1,0:T(8,128)(2,1)}, u32[]{:S(2)}, u32[]{:S(2)}) collective-permute-start(bf16[2,16,160,128]{3,2,1,0:T(8,128)(2,1)S(1)} %param.13), channel_id=1, source_target_pairs={{0,112},{8,120},{16,96},{24,104},{32,80},{40,88},{48,64},{56,72},{... | collective-permute-start | bytes 3932168 | tf_op jit(solution)/shard_map/cond/branch_13_fun/ppermute | solution.py:93
  122.7 1.1 copy-start
